TPU v7x, 256 devices: a whole 4x4x8 slice. The times are simulated.
256 devices in a mesh: circ: 8 (over y_lo, x), span: 32 (over y_hi, z, core).
Axes of the slice: x: 4, y: 4 (y_hi: 2, y_lo: 2; y = y_hi * 2 + y_lo), z: 8, core: 2. Of those that a mesh axis runs over, the one named last changes fastest.
Arguments:
- q_old: float32 [5, 32, 4096, 128], P(None, 'circ', 'span'), may hold values from -6 to 6
- pseudo_rate: float32 [32, 4096, 128], P('circ', 'span'), may hold values from 0.15 to 0.45
- flux_jacobians: float32 [3, 5, 5], replicated, may hold values from -2.5 to 2.5
- rotor_face: float32 [5, 32, 4096], P(None, 'circ', 'span'), may hold values from -6 to 6
- offsets: int32 [4096], P('span'), may hold values from 0 to 31
- owners: int32 [8, 128, 4], P('circ', 'span'), may hold values from 0 to 31, all different within a row; in each aligned block of 4 rows (0 to 3, 4 to 7, ..., all dimensions but the last counted through in order) at most 2 rows name the same one
- slots: int32 [8, 128, 4], P('circ', 'span'), may hold values from 0 to 3
- weight_idx: int32 [8, 128, 4], P('circ', 'span'), may hold values from 0 to 15
- weight_table: float32 [16], replicated, may hold values from 0.3 to 1
Outputs:
- q_new: float32 [5, 32, 4096, 128], P(None, 'circ', 'span')
Inputs may be any that keep to these rules, and one draw needn't show every extreme that they name: The 4 owners of one rotor panel differ; among the 4 rotor panels of one device in one circumferential block, no owner is named more than 2 times, and that count is reached.
All inputs are finite; a program needn't handle non-finite values.
Results may differ from a plain program's by a relative error of at most 0.000068.
Values sent between devices are 32-bit elements; how exact they have to be, the bound alone decides.
No kernel may reach another device: no remote copies, remote signals or barrier semaphores. Data moves between devices by JAX's collectives and lax.ppermute only.
A program may use at most 64 MiB of HBM per device.

v0:
```python
import jax
import jax.numpy as jnp
from jax import lax
from jax.sharding import PartitionSpec as P

NF = 5
KP_DEV = 4
PW = 32
inv_step = 0.5
viscosity = 0.1


def with_halo(block, sides, width):
    for axis, dim in sides:
        count = lax.axis_size(axis)
        forward = [(i, i + 1) for i in range(count - 1)]
        forward.append((count - 1, 0))
        backward = [(target, source) for source, target in forward]
        low = lax.ppermute(
            lax.slice_in_dim(block, block.shape[dim] - width, None, axis=dim), axis, forward
        )
        high = lax.ppermute(lax.slice_in_dim(block, 0, width, axis=dim), axis, backward)
        block = jnp.concatenate([low, block, high], axis=dim)
    return block


def contract(matrix, values):
    return jnp.einsum("fg,gtsa->ftsa", matrix, values, precision=lax.Precision.HIGHEST)


def advance(padded, current, previous, rate_cells, inlet_plane, jacobians):
    circ_up = padded[:, 2:, 1:-1]
    circ_down = padded[:, :-2, 1:-1]
    span_up = padded[:, 1:-1, 2:]
    span_down = padded[:, 1:-1, :-2]
    zero_column = jnp.zeros_like(current[..., :1])
    axial_up = jnp.concatenate([current[..., 1:], zero_column], axis=-1)
    axial_down = jnp.concatenate([inlet_plane[..., None], current[..., :-1]], axis=-1)
    convection = contract(jacobians[0], circ_up - circ_down)
    convection = convection + contract(jacobians[1], span_up - span_down)
    convection = convection + contract(jacobians[2], axial_up - axial_down)
    laplacian = (
        circ_up + circ_down + (span_up + span_down) + (axial_up + axial_down) - 6.0 * current
    )
    residual = inv_step * (current - previous) + 0.5 * convection - viscosity * laplacian
    return current - rate_cells[None] * residual


def wall_zero(field_array, width):
    span_index = lax.axis_index("span")
    span_count = lax.axis_size("span")
    length = field_array.shape[2]
    position = jnp.arange(length, dtype=jnp.int32)
    at_hub = jnp.logical_and(span_index == 0, position < width)
    at_tip = jnp.logical_and(span_index == span_count - 1, position >= length - width)
    keeping = jnp.logical_not(jnp.logical_or(at_hub, at_tip)).astype(field_array.dtype)
    keeping = keeping.reshape(1, 1, length, 1)
    return field_array * keeping


def body(
    q_old, pseudo_rate, flux_jacobians, rotor_face, offsets, owners, slots, weight_idx, weight_table
):
    circ_count = lax.axis_size("circ")
    rows_local = rotor_face.shape[1]
    total_rows = rows_local * circ_count
    row_iota = jnp.arange(rows_local, dtype=jnp.int32)
    all_rows = lax.all_gather(rotor_face, "circ", axis=1, tiled=True)
    first_row = lax.axis_index("circ") * rows_local
    source_rows = (first_row + row_iota[:, None] - offsets[None, :]) % total_rows
    rotated = jnp.take_along_axis(all_rows, source_rows[None], axis=1)
    panels = rotated.reshape(NF, rows_local, KP_DEV, PW)
    table_ids = jnp.arange(weight_table.shape[0], dtype=jnp.int32)
    weights = jnp.sum(jnp.where(weight_idx[..., None] == table_ids, weight_table, 0.0), axis=-1)
    targets = owners[0] * KP_DEV + slots[0]
    local_weights = weights[0]
    panel_ids = jnp.arange(KP_DEV * lax.axis_size("span"), dtype=jnp.int32)
    mixing = jnp.sum(
        jnp.where(targets[None] == panel_ids[:, None, None], local_weights[None], 0.0), axis=-1
    )
    own_panels = lax.psum_scatter(
        jnp.einsum("gk,ftkp->gftp", mixing, panels, precision=lax.Precision.HIGHEST),
        "span",
        scatter_dimension=0,
        tiled=True,
    )
    inlet_plane = jnp.transpose(own_panels, (1, 2, 0, 3)).reshape(NF, rows_local, KP_DEV * PW)

    def sweep(current):
        padded = with_halo(current, (("circ", 1), ("span", 2)), 1)
        padded = wall_zero(padded, 1)
        return advance(padded, current, q_old, pseudo_rate, inlet_plane, flux_jacobians)

    first_pass = sweep(q_old)
    return sweep(first_pass)


def solution(mesh):
    return jax.shard_map(
        body,
        mesh=mesh,
        in_specs=(
            P(None, "circ", "span", None),
            P("circ", "span", None),
            P(),
            P(None, "circ", "span"),
            P("span"),
            P("circ", "span", None),
            P("circ", "span", None),
            P("circ", "span", None),
            P(),
        ),
        out_specs=P(None, "circ", "span", None),
        check_vma=False,
    )
```

profile of v0, /device:TPU:6, one launch (start us, length us, event | category | flops | bytes accessed | tf_op | source)
XLA Modules:
  0.0 389.9 jit_solution(16798565273600464727)
XLA Ops:
  6.5 0.0 all-reduce.5.cloned.1.call-start
  6.5 1.1 fusion.53
  7.7 1.0 copy.107
  8.7 1.6 collective-permute-start
  10.3 1.0 copy.108
  11.3 0.5 collective-permute-start.1
  11.9 0.0 copy-done.9
  11.9 0.1 sub.82
  11.9 0.1 fusion.43
  12.0 0.1 compare_and_fusion
  12.1 0.0 copy-done.4
  12.1 37.0 %all_gather.3 = f32[5,32,128]{2,0,1:T(8,128)S(1)} all-gather(f32[5,4,128]{2,0,1:T(8,128)S(1)} %copy.72), channel_id=1, replica_groups=mesh['circ'=8,'span'=32] {'circ'}, dimensions={1}, use_global_device_ids=true | all-gather | bytes 92160 | tf_op jit(solution)/shard_map/all_gather | solution.py:68
  49.1 0.6 copy.73
  49.8 0.0 copy-start
  49.8 5.9 %gather_fusion = f32[512,5]{1,0:T(8,128)} fusion(f32[5,32,128]{0,2,1:T(8,128)S(1)} %copy.73, s32[512]{0:T(512)S(1)} %fusion.43), kind=kCustom, calls=%fused_computation | custom fusion | bytes 24576 | tf_op jit(solution)/shard_map/jit(take_along_axis)/gather | solution.py:71
  55.7 1.1 copy.87
  56.8 0.0 copy-done.6
  56.8 0.0 copy-done.7
  56.9 0.0 copy-done.8
  56.9 0.0 copy-done.10
  56.9 0.2 select_reduce_fusion.1
  57.0 0.1 select_reduce_fusion
  57.1 2.3 fusion.34
  59.5 0.0 all-reduce.5.cloned.1.call-update
  59.5 0.0 copy-done
  59.5 1.5 fusion.54
  61.0 3.4 copy.106
  64.4 2.1 copy.105
  66.6 0.0 copy-done.11
  66.6 0.6 dynamic-slice
  67.8 0.0 copy-done.5
  67.9 264.7 %all-reduce.5.cloned.1.call-done = f32[128,5,4,32]{3,0,2,1:T(8,128)} async-done(((f32[128,5,4,32]{3,0,2,1:T(8,128)}), f32[128,5,4,32]{3,0,2,1:T(8,128)}) %all-reduce.5.cloned.1.call-update) | async-done | bytes 327696
  332.6 0.9 dynamic-slice_bitcast_fusion
  333.5 0.1 broadcast_in_dim_reshape.4
  333.6 0.7 copy.76
  334.3 0.0 collective-permute-done
  334.3 1.1 constant_dynamic-update-slice_fusion.1
  335.4 0.8 copy_dynamic-update-slice_fusion
  336.2 0.0 collective-permute-done.1
  336.2 1.5 constant_dynamic-update-slice_fusion
  337.8 0.2 collective-permute-start.2
  338.0 5.8 %collective-permute-start.3 = (f32[5,6,1,128]{3,0,2,1:T(8,128)S(1)}, f32[5,6,1,128]{3,0,2,1:T(8,128)S(1)}, u32[]{:S(2)}, u32[]{:S(2)}) collective-permute-start(f32[5,6,1,128]{3,0,2,1:T(8,128)S(1)} %get-tuple-element.8), channel_id=1, source_target_pairs={{1,0},{2,1},{3,2},{4,3},{5,4},{6,5},{7,6},{8,7},{9,8},{10,9},{11,1... | collective-permute-start | bytes 46088 | tf_op jit(solution)/shard_map/ppermute | solution.py:22
  343.8 2.5 fusion.18
  346.3 0.0 collective-permute-done.2
  346.3 0.0 collective-permute-done.3
  346.3 0.3 maximum_multiply_fusion
  346.6 0.0 copy-start.3
  346.6 2.0 fusion.20
  348.7 4.9 %fusion.7 = f32[5,4,128,128]{3,0,2,1:T(8,128)S(1)} fusion(f32[4,128,128,5]{2,3,1,0:T(8,128)S(1)} %fusion.18, f32[4,128,128,5]{2,3,1,0:T(8,128)S(1)} %fusion.20, f32[5,6,130,128]{3,0,2,1:T(8,128)S(1)} %maximum_multiply_fusion, f32[5,4,128,127]{3,0,2,1:T(8,128)S(1)} %copy-done.2, f32[4,128,128]{2,1,0:T(8,128)S(1)} %copy-done.3, ...), kind=kOutput, calls=%fused_computation.14 | convolution fusion | flops 25559040 | bytes 25954816 | tf_op jit(solution)/shard_map/fg,gtsa->ftsa/dot_general | solution.py:28
  353.6 0.1 fusion.51
  353.7 0.6 collective-permute-start.4
  354.3 1.5 collective-permute-start.5
  355.8 0.7 fusion.52
  356.5 6.5 %collective-permute-done.4 = f32[5,1,128,128]{3,0,2,1:T(8,128)S(1)} collective-permute-done((f32[5,1,128,128]{3,0,2,1:T(8,128)S(1)}, f32[5,1,128,128]{3,0,2,1:T(8,128)S(1)}, u32[]{:S(2)}, u32[]{:S(2)}) %collective-permute-start.4) | collective-permute-done | bytes 327712 | tf_op jit(solution)/shard_map/ppermute | solution.py:19
  362.9 2.7 collective-permute-done.5
  365.6 0.1 collective-permute-start.6
  365.7 6.1 %collective-permute-start.7 = (f32[5,6,1,128]{3,0,2,1:T(8,128)S(1)}, f32[5,6,1,128]{3,0,2,1:T(8,128)S(1)}, u32[]{:S(2)}, u32[]{:S(2)}) collective-permute-start(f32[5,6,1,128]{3,0,2,1:T(8,128)S(1)} %get-tuple-element.6), channel_id=1, source_target_pairs={{1,0},{2,1},{3,2},{4,3},{5,4},{6,5},{7,6},{8,7},{9,8},{10,9},{11,1... | collective-permute-start | bytes 46088 | tf_op jit(solution)/shard_map/ppermute | solution.py:22
  371.8 2.5 fusion.8
  374.3 0.0 collective-permute-done.6
  374.3 0.0 collective-permute-done.7
  374.3 0.4 maximum_multiply_fusion.1
  374.7 2.0 fusion.10
  376.7 5.0 %fusion.3 = f32[5,4,128,128]{3,0,2,1:T(8,128)S(1)} fusion(f32[5,4,128,128]{3,0,2,1:T(8,128)S(1)} %fusion.7, f32[4,128,128,5]{2,3,1,0:T(8,128)S(1)} %fusion.8, f32[4,128,128,5]{2,3,1,0:T(8,128)S(1)} %fusion.10, f32[5,6,130,128]{3,0,2,1:T(8,128)S(1)} %maximum_multiply_fusion.1, f32[5,4,128,127]{3,0,2,1:T(8,128)S(1)} %get-tuple-element.12, ...), kind=kOutput, calls=%fused_computation.9 | convolution fusion | flops 25559040 | bytes 28051968 | tf_op jit(solution)/shard_map/fg,gtsa->ftsa/dot_general | solution.py:28
  381.7 1.3 copy.82
  (20 shorter events, 0.1 us)
Async XLA Ops:
  6.5 5.3 %copy-start.9 = (s32[128]{0:T(128)S(1)}, s32[128]{0:T(128)}, u32[]{:S(2)}) copy-start(s32[128]{0:T(128)} %param.13) | copy-start | bytes 1540
  6.5 5.6 %copy-start.4 = (f32[5,4,128]{2,1,0:T(4,128)S(1)}, f32[5,4,128]{2,1,0:T(4,128)}, u32[]{:S(2)}) copy-start(f32[5,4,128]{2,1,0:T(4,128)} %param.12) | copy-start | bytes 30724
  6.5 326.1 %all-reduce.5.cloned.1.call-start = ((), (), s32[]{:S(2)}) async-start(), calls=%async_computation | async-start | bytes 2621440
  8.7 48.1 %copy-start.6 = (s32[1,4,4]{2,1,0:T(4,128)S(1)}, s32[1,4,4]{2,1,0:T(4,128)}, u32[]{:S(2)}) copy-start(s32[1,4,4]{2,1,0:T(4,128)} %param.15) | copy-start | bytes 196
  8.7 48.1 %copy-start.7 = (s32[1,4,4]{2,1,0:T(4,128)S(1)}, s32[1,4,4]{2,1,0:T(4,128)}, u32[]{:S(2)}) copy-start(s32[1,4,4]{2,1,0:T(4,128)} %param.14) | copy-start | bytes 196
  8.7 48.2 %copy-start.8 = (s32[1,4,4]{2,1,0:T(4,128)S(1)}, s32[1,4,4]{2,1,0:T(4,128)}, u32[]{:S(2)}) copy-start(s32[1,4,4]{2,1,0:T(4,128)} %param.16) | copy-start | bytes 196
  8.7 48.2 %copy-start.10 = (f32[16]{0:T(128)S(1)}, f32[16]{0:T(128)}, u32[]{:S(2)}) copy-start(f32[16]{0:T(128)} %param.17) | copy-start | bytes 196
  8.7 325.6 %collective-permute-start = (f32[5,1,128,128]{3,0,2,1:T(8,128)}, f32[5,1,128,128]{3,0,2,1:T(8,128)}, u32[]{:S(2)}, u32[]{:S(2)}) collective-permute-start(f32[5,1,128,128]{3,0,2,1:T(8,128)} %copy.107), channel_id=1, source_target_pairs={{0,32},{32,64},{64,96},{96,128},{128,160},{160,192},{192,224},{224... | collective-permute-start | bytes 983048 | tf_op jit(solution)/shard_map/ppermute | solution.py:19
  11.3 324.9 %collective-permute-start.1 = (f32[5,1,128,128]{3,0,2,1:T(8,128)}, f32[5,1,128,128]{3,0,2,1:T(8,128)}, u32[]{:S(2)}, u32[]{:S(2)}) collective-permute-start(f32[5,1,128,128]{3,0,2,1:T(8,128)} %copy.108), channel_id=1, source_target_pairs={{32,0},{64,32},{96,64},{128,96},{160,128},{192,160},{224,192},{0,2... | collective-permute-start | bytes 983048 | tf_op jit(solution)/shard_map/ppermute | solution.py:22
  49.8 9.7 %copy-start = (f32[5,4,128,128]{3,2,1,0:T(8,128)S(1)}, f32[5,4,128,128]{3,2,1,0:T(8,128)}, u32[]{:S(2)}) copy-start(f32[5,4,128,128]{3,2,1,0:T(8,128)} %param.9) | copy-start | bytes 3932164
  64.4 2.2 copy-start.11
  64.4 3.4 copy-start.5
  335.4 8.4 %copy-start.1 = (f32[5,4,128,127]{3,0,2,1:T(8,128)S(1)}, f32[5,4,128,127]{3,0,2,1:T(8,128)}, u32[]{:S(2)}) copy-start(f32[5,4,128,127]{3,0,2,1:T(8,128)} %copy.106) | copy-start | bytes 3901444
  335.4 8.4 %copy-start.2 = (f32[5,4,128,127]{3,0,2,1:T(8,128)S(1)}, f32[5,4,128,127]{3,0,2,1:T(8,128)}, u32[]{:S(2)}) copy-start(f32[5,4,128,127]{3,0,2,1:T(8,128)} %copy.105) | copy-start | bytes 3901444
  337.8 8.5 %collective-permute-start.2 = (f32[5,6,1,128]{3,0,2,1:T(8,128)S(1)}, f32[5,6,1,128]{3,0,2,1:T(8,128)S(1)}, u32[]{:S(2)}, u32[]{:S(2)}) collective-permute-start(f32[5,6,1,128]{3,0,2,1:T(8,128)S(1)} %get-tuple-element.7), channel_id=1, source_target_pairs={{0,1},{1,2},{2,3},{3,4},{4,5},{5,6},{6,7},{7,8},{8,9},{9,10},{10,1... | collective-permute-start | bytes 46088 | tf_op jit(solution)/shard_map/ppermute | solution.py:19
  338.0 8.3 %collective-permute-start.3 = (f32[5,6,1,128]{3,0,2,1:T(8,128)S(1)}, f32[5,6,1,128]{3,0,2,1:T(8,128)S(1)}, u32[]{:S(2)}, u32[]{:S(2)}) collective-permute-start(f32[5,6,1,128]{3,0,2,1:T(8,128)S(1)} %get-tuple-element.8), channel_id=1, source_target_pairs={{1,0},{2,1},{3,2},{4,3},{5,4},{6,5},{7,6},{8,7},{9,8},{10,9},{11,1... | collective-permute-start | bytes 46088 | tf_op jit(solution)/shard_map/ppermute | solution.py:22
  346.6 2.0 copy-start.3
  353.7 9.3 %collective-permute-start.4 = (f32[5,1,128,128]{3,0,2,1:T(8,128)S(1)}, f32[5,1,128,128]{3,0,2,1:T(8,128)S(1)}, u32[]{:S(2)}, u32[]{:S(2)}) collective-permute-start(f32[5,1,128,128]{3,0,2,1:T(8,128)S(1)} %get-tuple-element.9), channel_id=1, source_target_pairs={{0,32},{32,64},{64,96},{96,128},{128,160},{160,192},{192,224},{224... | collective-permute-start | bytes 983048 | tf_op jit(solution)/shard_map/ppermute | solution.py:19
  354.3 11.3 %collective-permute-start.5 = (f32[5,1,128,128]{3,0,2,1:T(8,128)S(1)}, f32[5,1,128,128]{3,0,2,1:T(8,128)S(1)}, u32[]{:S(2)}, u32[]{:S(2)}) collective-permute-start(f32[5,1,128,128]{3,0,2,1:T(8,128)S(1)} %get-tuple-element.10), channel_id=1, source_target_pairs={{32,0},{64,32},{96,64},{128,96},{160,128},{192,160},{224,192},{0,2... | collective-permute-start | bytes 983048 | tf_op jit(solution)/shard_map/ppermute | solution.py:22
  365.6 8.7 %collective-permute-start.6 = (f32[5,6,1,128]{3,0,2,1:T(8,128)S(1)}, f32[5,6,1,128]{3,0,2,1:T(8,128)S(1)}, u32[]{:S(2)}, u32[]{:S(2)}) collective-permute-start(f32[5,6,1,128]{3,0,2,1:T(8,128)S(1)} %get-tuple-element.5), channel_id=1, source_target_pairs={{0,1},{1,2},{2,3},{3,4},{4,5},{5,6},{6,7},{7,8},{8,9},{9,10},{10,1... | collective-permute-start | bytes 46088 | tf_op jit(solution)/shard_map/ppermute | solution.py:19
  365.7 8.6 %collective-permute-start.7 = (f32[5,6,1,128]{3,0,2,1:T(8,128)S(1)}, f32[5,6,1,128]{3,0,2,1:T(8,128)S(1)}, u32[]{:S(2)}, u32[]{:S(2)}) collective-permute-start(f32[5,6,1,128]{3,0,2,1:T(8,128)S(1)} %get-tuple-element.6), channel_id=1, source_target_pairs={{1,0},{2,1},{3,2},{4,3},{5,4},{6,5},{7,6},{8,7},{9,8},{10,9},{11,1... | collective-permute-start | bytes 46088 | tf_op jit(solution)/shard_map/ppermute | solution.py:22
Sparse Core Ops, SparseCore 0:
  59.6 272.9 all-reduce.4
where the time goes:
time: 390 us
  waiting for transfers between devices  274 us (70%)
  blocking collectives  37 us (9%)
  local copies, waits for them, and re-layouts  25.8 us (7%)
  matrix products  21.3 us (5%)
  starting transfers between devices  16.4 us (4%)
  between operations  14.4 us (4%)
    unnamed x2, waiting for transfers between devices  265 us
    all_gather x1, blocking collectives, body(): all_rows = lax.all_gather(rotor_face, 'circ', axis=1, tiled=True)  37 us
    dot_general x6, matrix products, contract(): jnp.einsum('fg,gtsa->ftsa', matrix, values, precision=lax.Precision.HIGHEST)  18.9 us
    ppermute x4, starting transfers between devices, with_halo(): lax.ppermute(lax.slice_in_dim(block, 0, width, axis=dim), axis, backward)  13.8 us
    unnamed x32, local copies, waits for them, and re-layouts  10.2 us
  transfers between devices with their start and end apart: 9, of which 3 were waited for; matrix products, arithmetic and copies ran while one was open for 7% of the time, Pallas kernels for 0%

commit v1 on v0

--- a/solution.py
+++ b/solution.py
@@ -2,6 +2,7 @@
 import jax.numpy as jnp
 from jax import lax
 from jax.sharding import PartitionSpec as P
+from jax.lax import all_to_all, axis_size
 
 NF = 5
 KP_DEV = 4
@@ -65,7 +66,9 @@
     rows_local = rotor_face.shape[1]
     total_rows = rows_local * circ_count
     row_iota = jnp.arange(rows_local, dtype=jnp.int32)
-    all_rows = lax.all_gather(rotor_face, "circ", axis=1, tiled=True)
+    local_out = jnp.stack([rotor_face for _ in range(axis_size("circ"))], axis=0)
+    current_value = all_to_all(local_out, axis_name="circ", split_axis=0, concat_axis=0)
+    all_rows = jnp.concatenate(current_value, 1)
     first_row = lax.axis_index("circ") * rows_local
     source_rows = (first_row + row_iota[:, None] - offsets[None, :]) % total_rows
     rotated = jnp.take_along_axis(all_rows, source_rows[None], axis=1)

time: 390 us -> 373 us (0.956)
  blocking collectives: 37 us -> 0 us
  matrix products: 21.3 us -> 27.2 us
  starting transfers between devices: 16.4 us -> 22.1 us
  local copies, waits for them, and re-layouts: 25.8 us -> 30.1 us
    all_gather x1 -> x0, blocking collectives: 37 us -> none  [body(): all_rows = lax.all_gather(rotor_face, 'circ', axis=1, tiled=True)]
    dot_general x6, matrix products: 18.9 us -> 24.9 us  [contract(): jnp.einsum('fg,gtsa->ftsa', matrix, values, precision=lax.Precision.HIGHEST)]
    all_to_all x0 -> x1, starting transfers between devices: none -> 5.79 us  [body(): all_to_all(local_out, axis_name='circ', split_axis=0, concat_axis=0)]
    ppermute x4, waiting for transfers between devices: 6.49 us -> 11.3 us  [with_halo(): lax.ppermute(lax.slice_in_dim(block, block.shape[dim] - width, None, axis...]
    unnamed x32 -> x35, local copies, waits for them, and re-layouts: 10.2 us -> 13.5 us
  transfers between devices with their start and end apart: 9 -> 10, of which waited for: 3 -> 3; matrix products, arithmetic and copies ran while one was open for 7% -> 9% of each run, Pallas kernels for 0% -> 0%
where the time goes in v1:
time: 373 us
  waiting for transfers between devices  276 us (74%)
  local copies, waits for them, and re-layouts  30.1 us (8%)
  matrix products  27.2 us (7%)
  starting transfers between devices  22.1 us (6%)
  between operations  14.4 us (4%)
    unnamed x2, waiting for transfers between devices  262 us
    dot_general x6, matrix products, contract(): jnp.einsum('fg,gtsa->ftsa', matrix, values, precision=lax.Precision.HIGHEST)  24.9 us
    ppermute x4, starting transfers between devices, with_halo(): lax.ppermute(lax.slice_in_dim(block, 0, width, axis=dim), axis, backward)  13.8 us
    unnamed x35, local copies, waits for them, and re-layouts  13.5 us
    ppermute x4, waiting for transfers between devices, with_halo(): lax.ppermute(lax.slice_in_dim(block, block.shape[dim] - width, None, axis...  11.3 us
  transfers between devices with their start and end apart: 10, of which 3 were waited for; matrix products, arithmetic and copies ran while one was open for 9% of the time, Pallas kernels for 0%

profile of v1, /device:TPU:6, one launch (start us, length us, event | category | flops | bytes accessed | tf_op | source)
XLA Modules:
  0.0 372.8 jit_solution(6200574052720003767)
XLA Ops:
  6.5 1.5 stack.2
  8.0 5.8 %all-to-all-start = ((f32[8,5,4,128]{3,2,1,0:T(4,128)}), f32[8,5,4,128]{3,2,1,0:T(4,128)S(1)}, u32[]{:S(2)}, u32[]{:S(2)}) async-start(f32[8,5,4,128]{3,2,1,0:T(4,128)} %stack.2), calls=%async_computation | async-start | bytes 163840 | tf_op jit(solution)/shard_map/all_to_all | solution.py:70
  13.8 0.0 all-reduce.5.cloned.1.call-start
  13.8 1.1 fusion.53
  14.9 1.0 copy.105
  15.9 1.5 collective-permute-start
  17.4 1.0 copy.106
  18.4 0.6 collective-permute-start.1
  19.0 0.0 copy-done
  19.0 1.5 fusion.54
  20.5 0.0 copy-done.11
  20.5 0.1 sub.82
  20.6 0.0 copy-done.7
  20.6 3.5 copy.104
  24.0 0.0 copy-start.12
  24.1 2.2 copy.103
  26.2 0.0 copy-done.13
  26.2 0.6 dynamic-slice
  27.5 0.0 copy-done.8
  27.5 0.2 select_reduce_fusion.1
  27.7 0.1 select_reduce_fusion
  27.8 0.1 compare_and_fusion
  27.9 0.1 fusion.43
  28.0 0.0 all-to-all-done
  28.0 0.6 copy.71
  28.6 5.9 %gather_fusion = f32[512,5]{1,0:T(8,128)} fusion(f32[5,32,128]{0,2,1:T(8,128)S(1)} %bitcast.64, s32[512]{0:T(512)S(1)} %fusion.43), kind=kCustom, calls=%fused_computation | custom fusion | bytes 24576 | tf_op jit(solution)/shard_map/jit(take_along_axis)/gather | solution.py:74
  34.6 1.1 copy.85
  35.7 0.0 collective-permute-done
  35.7 1.1 constant_dynamic-update-slice_fusion.1
  36.8 0.8 copy_dynamic-update-slice_fusion
  37.6 0.0 collective-permute-done.1
  37.6 1.1 constant_dynamic-update-slice_fusion
  38.7 1.6 copy-done.5
  40.3 0.0 collective-permute-start.2
  40.3 6.8 %collective-permute-start.3 = (f32[5,6,1,128]{3,0,2,1:T(8,128)S(1)}, f32[5,6,1,128]{3,0,2,1:T(8,128)S(1)}, u32[]{:S(2)}, u32[]{:S(2)}) collective-permute-start(f32[5,6,1,128]{3,0,2,1:T(8,128)S(1)} %get-tuple-element.8), channel_id=1, source_target_pairs={{1,0},{2,1},{3,2},{4,3},{5,4},{6,5},{7,6},{8,7},{9,8},{10,9},{11,1... | collective-permute-start | bytes 46088 | tf_op jit(solution)/shard_map/ppermute | solution.py:23
  47.1 2.3 fusion.34
  49.4 0.0 all-reduce.5.cloned.1.call-update
  49.4 0.0 collective-permute-done.2
  49.4 0.0 collective-permute-done.3
  49.4 2.2 maximum_multiply_fusion
  51.7 1.6 copy-done.3
  53.3 3.4 fusion.20
  56.7 262.3 %all-reduce.5.cloned.1.call-done = f32[128,5,4,32]{3,0,2,1:T(8,128)} async-done(((f32[128,5,4,32]{3,0,2,1:T(8,128)}), f32[128,5,4,32]{3,0,2,1:T(8,128)}) %all-reduce.5.cloned.1.call-update) | async-done | bytes 327696
  319.0 0.9 dynamic-slice_bitcast_fusion
  319.9 0.1 broadcast_in_dim_reshape.4
  320.0 0.7 copy.74
  320.8 0.0 copy-start.6
  320.8 4.9 %fusion.18 = f32[4,128,128,5]{2,3,1,0:T(8,128)S(1)} fusion(f32[5,4,128,127]{3,0,2,1:T(8,128)} %copy.103, f32[5,4,128,127]{3,0,2,1:T(8,128)} %copy.104, f32[5,4,128,1]{3,0,2,1:T(8,128)S(1)} %copy.74, f32[1,5,5]{2,0,1:T(1,128)S(1)} %get-tuple-element.19), kind=kOutput, calls=%fused_computation.23 | convolution fusion | flops 20316160 | bytes 3922020 | tf_op jit(solution)/shard_map/fg,gtsa->ftsa/dot_general | solution.py:29
  325.7 7.1 %fusion.7 = f32[5,4,128,128]{3,0,2,1:T(8,128)S(1)} fusion(f32[4,128,128,5]{2,3,1,0:T(8,128)S(1)} %fusion.18, f32[4,128,128,5]{2,3,1,0:T(8,128)} %fusion.20, f32[5,6,130,128]{3,0,2,1:T(8,128)S(1)} %copy-done.4, f32[5,4,128,127]{3,0,2,1:T(8,128)S(1)} %copy-done.2, f32[4,128,128]{2,1,0:T(8,128)S(1)} %copy-done.6, f32[5,4,128,128]{3,2,1,0:T(8,128)S(1)} %copy-done, ...), kind=kOutput, calls=%fused_computation.14 | convolution fusion | flops 25559040 | bytes 25168384 | tf_op jit(solution)/shard_map/fg,gtsa->ftsa/dot_general | solution.py:29
  332.8 0.1 fusion.51
  332.9 1.0 collective-permute-start.4
  333.9 1.1 collective-permute-start.5
  335.0 0.7 fusion.52
  335.7 11.3 %collective-permute-done.4 = f32[5,1,128,128]{3,0,2,1:T(8,128)S(1)} collective-permute-done((f32[5,1,128,128]{3,0,2,1:T(8,128)S(1)}, f32[5,1,128,128]{3,0,2,1:T(8,128)S(1)}, u32[]{:S(2)}, u32[]{:S(2)}) %collective-permute-start.4) | collective-permute-done | bytes 327712 | tf_op jit(solution)/shard_map/ppermute | solution.py:20
  347.0 2.4 collective-permute-done.5
  349.4 0.1 collective-permute-start.6
  349.4 5.3 %collective-permute-start.7 = (f32[5,6,1,128]{3,0,2,1:T(8,128)S(1)}, f32[5,6,1,128]{3,0,2,1:T(8,128)S(1)}, u32[]{:S(2)}, u32[]{:S(2)}) collective-permute-start(f32[5,6,1,128]{3,0,2,1:T(8,128)S(1)} %get-tuple-element.6), channel_id=1, source_target_pairs={{1,0},{2,1},{3,2},{4,3},{5,4},{6,5},{7,6},{8,7},{9,8},{10,9},{11,1... | collective-permute-start | bytes 46088 | tf_op jit(solution)/shard_map/ppermute | solution.py:23
  354.8 2.5 fusion.8
  357.3 0.0 collective-permute-done.6
  357.3 0.0 collective-permute-done.7
  357.3 0.3 maximum_multiply_fusion.1
  357.7 2.0 fusion.10
  359.7 5.0 %fusion.3 = f32[5,4,128,128]{3,0,2,1:T(8,128)S(1)} fusion(f32[5,4,128,128]{3,0,2,1:T(8,128)S(1)} %fusion.7, f32[4,128,128,5]{2,3,1,0:T(8,128)S(1)} %fusion.8, f32[4,128,128,5]{2,3,1,0:T(8,128)S(1)} %fusion.10, f32[5,6,130,128]{3,0,2,1:T(8,128)S(1)} %maximum_multiply_fusion.1, f32[5,4,128,127]{3,0,2,1:T(8,128)S(1)} %get-tuple-element.12, ...), kind=kOutput, calls=%fused_computation.9 | convolution fusion | flops 25559040 | bytes 28051968 | tf_op jit(solution)/shard_map/fg,gtsa->ftsa/dot_general | solution.py:29
  364.7 1.3 copy.80
  (25 shorter events, 0.1 us)
Async XLA Ops:
  6.5 12.4 %copy-start = (f32[5,4,128,128]{3,2,1,0:T(8,128)S(1)}, f32[5,4,128,128]{3,2,1,0:T(8,128)}, u32[]{:S(2)}) copy-start(f32[5,4,128,128]{3,2,1,0:T(8,128)} %param.9) | copy-start | bytes 3932164
  8.0 20.0 %all-to-all-start = ((f32[8,5,4,128]{3,2,1,0:T(4,128)}), f32[8,5,4,128]{3,2,1,0:T(4,128)S(1)}, u32[]{:S(2)}, u32[]{:S(2)}) async-start(f32[8,5,4,128]{3,2,1,0:T(4,128)} %stack.2), calls=%async_computation | async-start | bytes 163840 | tf_op jit(solution)/shard_map/all_to_all | solution.py:70
  13.8 305.3 %all-reduce.5.cloned.1.call-start = ((), (), s32[]{:S(2)}) async-start(), calls=%async_computation.1 | async-start | bytes 2621440
  15.9 19.8 %collective-permute-start = (f32[5,1,128,128]{3,0,2,1:T(8,128)}, f32[5,1,128,128]{3,0,2,1:T(8,128)}, u32[]{:S(2)}, u32[]{:S(2)}) collective-permute-start(f32[5,1,128,128]{3,0,2,1:T(8,128)} %copy.105), channel_id=1, source_target_pairs={{0,32},{32,64},{64,96},{96,128},{128,160},{160,192},{192,224},{224... | collective-permute-start | bytes 983048 | tf_op jit(solution)/shard_map/ppermute | solution.py:20
  18.4 19.2 %collective-permute-start.1 = (f32[5,1,128,128]{3,0,2,1:T(8,128)}, f32[5,1,128,128]{3,0,2,1:T(8,128)}, u32[]{:S(2)}, u32[]{:S(2)}) collective-permute-start(f32[5,1,128,128]{3,0,2,1:T(8,128)} %copy.106), channel_id=1, source_target_pairs={{32,0},{64,32},{96,64},{128,96},{160,128},{192,160},{224,192},{0,2... | collective-permute-start | bytes 983048 | tf_op jit(solution)/shard_map/ppermute | solution.py:23
  19.0 1.5 copy-start.11
  19.0 1.6 copy-start.7
  24.0 2.2 copy-start.13
  24.0 3.4 copy-start.8
  24.0 3.4 copy-start.9
  24.0 3.5 copy-start.10
  24.0 3.5 copy-start.12
  38.7 1.6 copy-start.5
  40.3 9.1 %collective-permute-start.2 = (f32[5,6,1,128]{3,0,2,1:T(8,128)S(1)}, f32[5,6,1,128]{3,0,2,1:T(8,128)S(1)}, u32[]{:S(2)}, u32[]{:S(2)}) collective-permute-start(f32[5,6,1,128]{3,0,2,1:T(8,128)S(1)} %get-tuple-element.7), channel_id=1, source_target_pairs={{0,1},{1,2},{2,3},{3,4},{4,5},{5,6},{6,7},{7,8},{8,9},{9,10},{10,1... | collective-permute-start | bytes 46088 | tf_op jit(solution)/shard_map/ppermute | solution.py:20
  40.3 9.1 %collective-permute-start.3 = (f32[5,6,1,128]{3,0,2,1:T(8,128)S(1)}, f32[5,6,1,128]{3,0,2,1:T(8,128)S(1)}, u32[]{:S(2)}, u32[]{:S(2)}) collective-permute-start(f32[5,6,1,128]{3,0,2,1:T(8,128)S(1)} %get-tuple-element.8), channel_id=1, source_target_pairs={{1,0},{2,1},{3,2},{4,3},{5,4},{6,5},{7,6},{8,7},{9,8},{10,9},{11,1... | collective-permute-start | bytes 46088 | tf_op jit(solution)/shard_map/ppermute | solution.py:23
  51.7 1.7 copy-start.3
  320.7 4.9 %copy-start.1 = (f32[5,4,128,127]{3,0,2,1:T(8,128)S(1)}, f32[5,4,128,127]{3,0,2,1:T(8,128)}, u32[]{:S(2)}) copy-start(f32[5,4,128,127]{3,0,2,1:T(8,128)} %copy.104) | copy-start | bytes 3901444
  320.8 4.9 %copy-start.2 = (f32[5,4,128,127]{3,0,2,1:T(8,128)S(1)}, f32[5,4,128,127]{3,0,2,1:T(8,128)}, u32[]{:S(2)}) copy-start(f32[5,4,128,127]{3,0,2,1:T(8,128)} %copy.103) | copy-start | bytes 3901444
  320.8 4.9 %copy-start.4 = (f32[5,6,130,128]{3,0,2,1:T(8,128)S(1)}, f32[5,6,130,128]{3,0,2,1:T(8,128)}, u32[]{:S(2)}) copy-start(f32[5,6,130,128]{3,0,2,1:T(8,128)} %copy-done.3) | copy-start | bytes 5990404
  320.8 4.9 %copy-start.6 = (f32[4,128,128]{2,1,0:T(8,128)S(1)}, f32[4,128,128]{2,1,0:T(8,128)}, u32[]{:S(2)}) copy-start(f32[4,128,128]{2,1,0:T(8,128)} %param.10) | copy-start | bytes 786436
  332.9 14.1 %collective-permute-start.4 = (f32[5,1,128,128]{3,0,2,1:T(8,128)S(1)}, f32[5,1,128,128]{3,0,2,1:T(8,128)S(1)}, u32[]{:S(2)}, u32[]{:S(2)}) collective-permute-start(f32[5,1,128,128]{3,0,2,1:T(8,128)S(1)} %get-tuple-element.9), channel_id=1, source_target_pairs={{0,32},{32,64},{64,96},{96,128},{128,160},{160,192},{192,224},{224... | collective-permute-start | bytes 983048 | tf_op jit(solution)/shard_map/ppermute | solution.py:20
  333.9 15.5 %collective-permute-start.5 = (f32[5,1,128,128]{3,0,2,1:T(8,128)S(1)}, f32[5,1,128,128]{3,0,2,1:T(8,128)S(1)}, u32[]{:S(2)}, u32[]{:S(2)}) collective-permute-start(f32[5,1,128,128]{3,0,2,1:T(8,128)S(1)} %get-tuple-element.10), channel_id=1, source_target_pairs={{32,0},{64,32},{96,64},{128,96},{160,128},{192,160},{224,192},{0,2... | collective-permute-start | bytes 983048 | tf_op jit(solution)/shard_map/ppermute | solution.py:23
  349.4 7.9 %collective-permute-start.6 = (f32[5,6,1,128]{3,0,2,1:T(8,128)S(1)}, f32[5,6,1,128]{3,0,2,1:T(8,128)S(1)}, u32[]{:S(2)}, u32[]{:S(2)}) collective-permute-start(f32[5,6,1,128]{3,0,2,1:T(8,128)S(1)} %get-tuple-element.5), channel_id=1, source_target_pairs={{0,1},{1,2},{2,3},{3,4},{4,5},{5,6},{6,7},{7,8},{8,9},{9,10},{10,1... | collective-permute-start | bytes 46088 | tf_op jit(solution)/shard_map/ppermute | solution.py:20
  349.4 7.8 %collective-permute-start.7 = (f32[5,6,1,128]{3,0,2,1:T(8,128)S(1)}, f32[5,6,1,128]{3,0,2,1:T(8,128)S(1)}, u32[]{:S(2)}, u32[]{:S(2)}) collective-permute-start(f32[5,6,1,128]{3,0,2,1:T(8,128)S(1)} %get-tuple-element.6), channel_id=1, source_target_pairs={{1,0},{2,1},{3,2},{4,3},{5,4},{6,5},{7,6},{8,7},{9,8},{10,9},{11,1... | collective-permute-start | bytes 46088 | tf_op jit(solution)/shard_map/ppermute | solution.py:23
Sparse Core Ops, SparseCore 0:
  49.5 269.4 all-reduce.4
